TPU v7x, 32 devices: a whole 2x2x4 slice. The times are simulated.
32 devices in a mesh: freq: 2 (over x), row: 4 (over z), col: 4 (over y, core).
Axes of the slice: x: 2, y: 2, z: 4, core: 2. Of those that a mesh axis runs over, the one named last changes fastest.
Arguments:
- sky_maps: bfloat16 [512, 128, 512], P('freq', 'row', 'col'), may hold values from -32 to 32
- beam_sigma: float32 [512], P('freq'), may hold values from 1.5 to 4
- whitening: bfloat16 [512, 512], replicated, may hold values from -0.25 to 0.25
- unmix_init: float32 [128, 512], replicated, may hold values from -0.25 to 0.25
Outputs:
- unmixing: float32 [128, 512], replicated
- sources: bfloat16 [128, 65536], P(None, ('freq', 'row', 'col'))
All inputs are finite; a program needn't handle non-finite values.
Results may differ from a plain program's by a relative error of at most 0.0025.
The roundings to bfloat16 on the way count: a program that leaves them out, or rounds other values in their place, can miss the bound.
Values may be sent and summed in bfloat16 or wider, within the bound.
No kernel may reach another device: no remote copies, remote signals or barrier semaphores. Data moves between devices by JAX's collectives and lax.ppermute only.
A program may use at most 64 MiB of HBM per device.

v0:
```python
import jax
import jax.numpy as jnp
from jax import lax
from jax.sharding import PartitionSpec as P

HALF = 8
ITERS = 2
NS_STEPS = 5


def with_halo(cells, sides, width):
    for axis, dim in sides:
        count = lax.axis_size(axis)
        ends = count - 1
        head = lax.slice_in_dim(cells, 0, width, axis=dim)
        tail = lax.slice_in_dim(cells, cells.shape[dim] - width, cells.shape[dim], axis=dim)
        cells = jnp.concatenate(
            [
                lax.ppermute(tail, axis, [(i, (i + 1) % count) for i in range(ends)]),
                cells,
                lax.ppermute(head, axis, [((i + 1) % count, i) for i in range(ends)]),
            ],
            axis=dim,
        )
    return cells


def make_taps(beam_sigma):
    offsets = jnp.arange(2 * HALF + 1, dtype=jnp.float32) - HALF
    shaped = jnp.exp(
        -(offsets[None, :] * offsets[None, :]) / (2.0 * beam_sigma[:, None] * beam_sigma[:, None])
    )
    return (shaped / jnp.sum(shaped, axis=1, keepdims=True)).astype(jnp.bfloat16)


def make_band(beam_taps, length):
    spread = beam_taps.shape[1]
    offsets = jnp.arange(length + spread - 1)[None, :] - jnp.arange(length)[:, None]
    onehot = (offsets[:, :, None] == jnp.arange(spread)[None, None, :]).astype(jnp.float32)
    return jnp.einsum("ijk,ck->cij", onehot, beam_taps.astype(jnp.float32)).astype(jnp.bfloat16)


def inverse_root(matrix):
    frob_norm = jnp.sqrt(jnp.sum(matrix * matrix) + 1e-06)
    current = matrix / frob_norm
    unit_matrix = jnp.eye(matrix.shape[0], dtype=jnp.float32)
    inverse = unit_matrix
    for iteration in range(NS_STEPS):
        correction = 0.5 * (
            3.0 * unit_matrix - jnp.dot(inverse, current, precision=lax.Precision.HIGHEST)
        )
        current = jnp.dot(current, correction, precision=lax.Precision.HIGHEST)
        inverse = jnp.dot(correction, inverse, precision=lax.Precision.HIGHEST)
    return inverse / jnp.sqrt(frob_norm)


def pixel_moments(coarse, whitened):
    outputs = jnp.dot(coarse, whitened, preferred_element_type=jnp.float32)
    cubed = (outputs * outputs * outputs).astype(jnp.bfloat16)
    return lax.dot_general(
        cubed, whitened, (((1,), (1,)), ((), ())), preferred_element_type=jnp.float32
    )


def shards(sky_maps, beam_sigma, whitening, unmix_init):
    beam_taps = make_taps(beam_sigma)
    channels, height, breadth = sky_maps.shape
    band_rows = make_band(beam_taps, height)
    band_cols = make_band(beam_taps, breadth)
    padded = with_halo(sky_maps, (("row", 1),), HALF)
    rowwise = jnp.einsum(
        "cik,ckj->cij", band_rows, padded, preferred_element_type=jnp.float32
    ).astype(jnp.bfloat16)
    widened = with_halo(rowwise, (("col", 2),), HALF)
    smoothed = jnp.einsum(
        "cim,cjm->cij", widened, band_cols, preferred_element_type=jnp.float32
    ).astype(jnp.bfloat16)
    plane_sums = lax.psum(jnp.sum(smoothed, axis=(1, 2), dtype=jnp.float32), ("row", "col"))
    flattened = smoothed.reshape(channels, height * breadth)
    spectra = lax.all_to_all(flattened, "freq", split_axis=1, concat_axis=0, tiled=True)
    devices = lax.axis_size("freq") * lax.axis_size("row") * lax.axis_size("col")
    total_pixels = spectra.shape[1] * devices
    channel_sums = lax.all_gather(plane_sums, "freq", axis=0, tiled=True)
    means = channel_sums / total_pixels
    shift = jnp.dot(whitening.astype(jnp.float32), means, precision=lax.Precision.HIGHEST)
    whitened = (
        jnp.dot(whitening, spectra, preferred_element_type=jnp.float32) - shift[:, None]
    ).astype(jnp.bfloat16)
    unmixing = unmix_init
    for iteration in range(ITERS):
        moments = pixel_moments(unmixing.astype(jnp.bfloat16), whitened)
        moments = lax.psum(moments, ("freq", "row", "col"))
        updated = moments / total_pixels - 3.0 * unmixing
        gram = jnp.dot(updated, updated.T, precision=lax.Precision.HIGHEST)
        unmixing = jnp.dot(inverse_root(gram), updated, precision=lax.Precision.HIGHEST)
    sources = jnp.dot(
        unmixing.astype(jnp.bfloat16), whitened, preferred_element_type=jnp.float32
    ).astype(jnp.bfloat16)
    return (unmixing, sources)


def solution(mesh):
    return jax.shard_map(
        shards,
        mesh=mesh,
        in_specs=(P("freq", "row", "col"), P("freq"), P(), P()),
        out_specs=(P(), P(None, ("freq", "row", "col"))),
        check_vma=False,
    )
```

profile of v0, /device:TPU:0, one launch (start us, length us, event | category | flops | bytes accessed | tf_op | source)
XLA Modules:
  0.0 394.4 jit_solution(6294452238984527691)
XLA Ops:
  7.2 1.3 fusion.76
  8.5 5.0 %collective-permute-start = (bf16[256,8,128]{2,1,0:T(8,128)(2,1)S(1)}, bf16[256,8,128]{2,1,0:T(8,128)(2,1)S(1)}, u32[]{:S(2)}, u32[]{:S(2)}) collective-permute-start(bf16[256,8,128]{2,1,0:T(8,128)(2,1)S(1)} %get-tuple-element.4), channel_id=1, source_target_pairs={{0,4},{4,8},{8,12},{1,5},{5,9},{9,13},{2,6},{6,10},{10,14},{3,7},{... | collective-permute-start | bytes 1572872 | tf_op jit(solution)/shard_map/ppermute | solution.py:19
  13.5 1.3 collective-permute-start.1
  14.9 0.1 fusion.55
  15.0 0.4 convolution_convert_fusion.2
  15.4 3.8 copy.7
  19.2 5.4 %collective-permute-done = bf16[256,8,128]{2,1,0:T(8,128)(2,1)S(1)} collective-permute-done((bf16[256,8,128]{2,1,0:T(8,128)(2,1)S(1)}, bf16[256,8,128]{2,1,0:T(8,128)(2,1)S(1)}, u32[]{:S(2)}, u32[]{:S(2)}) %collective-permute-start) | collective-permute-done | bytes 524320 | tf_op jit(solution)/shard_map/ppermute | solution.py:19
  24.6 4.3 %collective-permute-done.1 = bf16[256,8,128]{2,1,0:T(8,128)(2,1)} collective-permute-done((bf16[256,8,128]{2,1,0:T(8,128)(2,1)S(1)}, bf16[256,8,128]{2,1,0:T(8,128)(2,1)}, u32[]{:S(2)}, u32[]{:S(2)}) %collective-permute-start.1) | collective-permute-done | bytes 524320 | tf_op jit(solution)/shard_map/ppermute | solution.py:21
  28.9 3.3 fusion.13
  32.2 2.9 fusion.75
  35.1 2.7 copy.8
  37.8 2.7 copy.9
  40.5 1.3 collective-permute-start.3
  41.8 3.0 collective-permute-start.2
  44.9 5.2 %convolution_convert_fusion = bf16[256,128,144]{1,0,2:T(8,128)(2,1)} fusion(s32[128,144]{0,1:T(8,128)S(1)} %iota_subtract_fusion, f32[256]{0:T(256)S(1)} %fusion.55, f32[256]{0:T(256)S(1)} %multiply_multiply_fusion.2, f32[17]{0:T(128)S(1)} %multiply_negate_fusion), kind=kOutput, calls=%fused_computation.2 | convolution fusion | flops 165477120 | bytes 9513028 | tf_op jit(solution)/shard_map/ijk,ck->cij/dot_general | solution.py:40
  50.1 3.7 copy.10
  53.8 3.7 copy.11
  57.5 17.0 %convert_reduce_fusion = (f32[256]{0:T(256)S(1)}, bf16[256,32,128]{2,1,0:T(8,128)(2,1)}) fusion(bf16[256,128,144]{1,0,2:T(8,128)(2,1)} %convolution_convert_fusion, bf16[256,32,8]{2,1,0:T(8,128)(2,1)} %copy.11, bf16[256,32,128]{2,1,0:T(8,128)(2,1)S(1)} %fusion.13, bf16[256,32,8]{2,1,0:T(8,128)(2,1)} %copy.10), kind=kOutput, calls=%fused_computation.9 | convolution fusion | flops 312213248 | bytes 13894656 | tf_op jit(solution)/shard_map/cim,cjm->cij/dot_general | solution.py:75
  74.4 2.5 all_to_all.14
  77.0 2.2 copy.13
  79.2 3.8 all-to-all-start
  83.0 30.9 %psum.21 = f32[256]{0:T(256)S(1)} all-reduce(f32[256]{0:T(256)S(1)} %get-tuple-element.6), channel_id=1, replica_groups=mesh['freq'=2,'row'=4,'col'=4] {'row','col'}, use_global_device_ids=true, to_apply=%region_2.0 | all-reduce | flops 256 | bytes 2048 | tf_op jit(solution)/shard_map/psum | solution.py:78
  113.9 4.5 %all-gather = f32[2,1,256]{2,1,0:T(1,128)S(1)} all-gather(f32[1,1,256]{2,1,0:T(1,128)S(1)} %bitcast.82), channel_id=1, replica_groups=mesh['freq'=2,'row'=4,'col'=4] {'freq'}, dimensions={0}, use_global_device_ids=true | all-gather | bytes 3072 | tf_op jit(solution)/shard_map/all_gather | solution.py:83
  118.3 0.5 fusion.77
  118.8 1.3 copy-done.2
  120.2 2.9 subtract_convert_fusion
  123.2 1.9 fusion.22
  125.1 0.0 all-reduce.5.cloned.1.call-start
  125.1 122.5 %all-reduce.3.cloned.1.call-done = f32[128,512]{1,0:T(8,128)} async-done(((f32[128,512]{1,0:T(8,128)}), f32[128,512]{1,0:T(8,128)}) %all-reduce.3.cloned.1.call-update) | async-done | bytes 262160 | tf_op jit(solution)/shard_map/psum | solution.py:92
  247.6 2.1 multiply_reduce_fusion.1
  250.4 0.2 fusion.32
  250.6 0.2 fusion.53
  250.8 0.2 fusion.52
  251.0 0.2 fusion.31
  251.2 0.2 fusion.79
  251.5 0.2 fusion.78
  251.7 0.2 fusion.30
  251.9 0.2 fusion.81
  252.1 0.2 fusion.80
  252.3 0.2 fusion.29
  252.5 0.2 fusion.82
  252.7 0.2 fusion.83
  252.9 0.2 fusion.28
  253.2 0.2 convolution_divide_fusion.1
  253.4 0.4 fusion.47
  253.8 1.8 fusion.35
  255.6 124.1 %all-reduce.5.cloned.1.call-done = f32[128,512]{1,0:T(8,128)} async-done(((f32[128,512]{1,0:T(8,128)}), f32[128,512]{1,0:T(8,128)}) %all-reduce.5.cloned.1.call-update) | async-done | bytes 262160 | tf_op jit(solution)/shard_map/psum | solution.py:92
  379.7 2.1 multiply_reduce_fusion
  382.6 0.2 fusion.27
  382.8 0.2 fusion.54
  383.0 0.2 fusion.51
  383.2 0.2 fusion.26
  383.4 0.2 fusion.85
  383.6 0.2 fusion.84
  383.8 0.2 fusion.25
  384.0 0.2 fusion.87
  384.2 0.2 fusion.86
  384.4 0.2 fusion.24
  384.6 0.2 fusion.88
  384.9 0.2 fusion.89
  385.1 0.2 fusion.23
  385.3 0.2 convolution_divide_fusion
  385.5 0.4 fusion.49
  385.9 1.6 convolution_convert_fusion.1
  (24 shorter events, 0.1 us)
Async XLA Ops:
  7.2 111.2 %copy-start = (bf16[512,512]{1,0:T(8,128)(2,1)S(1)}, bf16[512,512]{1,0:T(8,128)(2,1)}, u32[]{:S(2)}) copy-start(bf16[512,512]{1,0:T(8,128)(2,1)} %param.6) | copy-start | bytes 1572868
  7.2 7.6 %copy-start.6 = (f32[256]{0:T(256)S(1)}, f32[256]{0:T(256)}, u32[]{:S(2)}) copy-start(f32[256]{0:T(256)} %param.5) | copy-start | bytes 3076
  8.5 16.1 %collective-permute-start = (bf16[256,8,128]{2,1,0:T(8,128)(2,1)S(1)}, bf16[256,8,128]{2,1,0:T(8,128)(2,1)S(1)}, u32[]{:S(2)}, u32[]{:S(2)}) collective-permute-start(bf16[256,8,128]{2,1,0:T(8,128)(2,1)S(1)} %get-tuple-element.4), channel_id=1, source_target_pairs={{0,4},{4,8},{8,12},{1,5},{5,9},{9,13},{2,6},{6,10},{10,14},{3,7},{... | collective-permute-start | bytes 1572872 | tf_op jit(solution)/shard_map/ppermute | solution.py:19
  13.5 15.4 %collective-permute-start.1 = (bf16[256,8,128]{2,1,0:T(8,128)(2,1)S(1)}, bf16[256,8,128]{2,1,0:T(8,128)(2,1)}, u32[]{:S(2)}, u32[]{:S(2)}) collective-permute-start(bf16[256,8,128]{2,1,0:T(8,128)(2,1)S(1)} %get-tuple-element.5), channel_id=1, source_target_pairs={{4,0},{8,4},{12,8},{5,1},{9,5},{13,9},{6,2},{10,6},{14,10},{7,3},{... | collective-permute-start | bytes 1572872 | tf_op jit(solution)/shard_map/ppermute | solution.py:21
  40.5 13.3 %collective-permute-start.3 = (bf16[256,32,8]{0,2,1:T(8,128)(2,1)S(1)}, bf16[256,32,8]{0,2,1:T(8,128)(2,1)S(1)}, u32[]{:S(2)}, u32[]{:S(2)}) collective-permute-start(bf16[256,32,8]{0,2,1:T(8,128)(2,1)S(1)} %copy.9), channel_id=1, source_target_pairs={{1,0},{2,1},{3,2},{5,4},{6,5},{7,6},{9,8},{10,9},{11,10},{13,12},{... | collective-permute-start | bytes 393224 | tf_op jit(solution)/shard_map/ppermute | solution.py:21
  41.8 8.2 %collective-permute-start.2 = (bf16[256,32,8]{0,2,1:T(8,128)(2,1)S(1)}, bf16[256,32,8]{0,2,1:T(8,128)(2,1)S(1)}, u32[]{:S(2)}, u32[]{:S(2)}) collective-permute-start(bf16[256,32,8]{0,2,1:T(8,128)(2,1)S(1)} %copy.8), channel_id=1, source_target_pairs={{0,1},{1,2},{2,3},{4,5},{5,6},{6,7},{8,9},{9,10},{10,11},{12,13},{... | collective-permute-start | bytes 393224 | tf_op jit(solution)/shard_map/ppermute | solution.py:19
  79.2 39.6 %all-to-all-start = ((bf16[256,2,2048]{2,0,1:T(8,128)(2,1)}), bf16[256,2,2048]{2,0,1:T(8,128)(2,1)S(1)}, u32[]{:S(2)}, u32[]{:S(2)}) async-start(bf16[256,2,2048]{2,0,1:T(8,128)(2,1)} %copy.13), calls=%async_computation | async-start | bytes 4194304 | tf_op jit(solution)/shard_map/all_to_all | solution.py:80
  83.0 164.6 %all-reduce.3.cloned.1.call-start = ((), (), s32[]{:S(2)}) async-start(), calls=%async_computation.1 | async-start | bytes 524288 | tf_op jit(solution)/shard_map/psum | solution.py:92
  118.8 1.4 copy-start.2
  120.2 3.0 copy-start.1
  125.1 254.7 %all-reduce.5.cloned.1.call-start = ((), (), s32[]{:S(2)}) async-start(), calls=%async_computation.2 | async-start | bytes 524288 | tf_op jit(solution)/shard_map/psum | solution.py:92
  247.6 5.8 %copy-start.3 = (f32[128,512]{1,0:T(8,128)S(1)}, f32[128,512]{1,0:T(8,128)}, u32[]{:S(2)}) copy-start(f32[128,512]{1,0:T(8,128)} %all-reduce.3.cloned.1.call-done) | copy-start | bytes 786436
  379.7 5.8 %copy-start.4 = (f32[128,512]{1,0:T(8,128)S(1)}, f32[128,512]{1,0:T(8,128)}, u32[]{:S(2)}) copy-start(f32[128,512]{1,0:T(8,128)} %all-reduce.5.cloned.1.call-done) | copy-start | bytes 786436
  385.9 1.6 copy-start.5
Sparse Core Ops, SparseCore 0:
  125.2 122.3 all-reduce.2
  255.7 123.9 all-reduce.4
where the time goes:
time: 395 us; the launch traced here: 394 us
  waiting for transfers between devices  256 us (65%)
  matrix products  45.3 us (11%)
  blocking collectives  35.3 us (9%)
  local copies, waits for them, and re-layouts  27 us (7%)
  between operations  15.9 us (4%)
  starting transfers between devices  14.4 us (4%)
    psum x2, waiting for transfers between devices, shards(): moments = lax.psum(moments, ('freq', 'row', 'col'))  247 us
    psum x1, blocking collectives, shards(): lax.psum(jnp.sum(smoothed, axis=(1, 2), dtype=jnp.float32), ('row', 'col'))  30.9 us
    dot_general x1, matrix products, shards(): jnp.einsum('cim,cjm->cij', widened, band_cols, preferred_element_type=jnp...  17 us
    ppermute x2, starting transfers between devices, with_halo(): lax.ppermute(tail, axis, [(i, (i + 1) % count) for i in range(ends)])  8 us
  transfers between devices with their start and end apart: 7, of which 4 were waited for; matrix products, arithmetic and copies ran while one was open for 3% of the time, Pallas kernels for 0%

commit v1 on v0

--- a/solution.py
+++ b/solution.py
@@ -89,7 +89,13 @@
     unmixing = unmix_init
     for iteration in range(ITERS):
         moments = pixel_moments(unmixing.astype(jnp.bfloat16), whitened)
-        moments = lax.psum(moments, ("freq", "row", "col"))
+
+        def handle_members_all(array_here):
+            for hop_no in (("row", "col"), "freq"):
+                array_here = lax.psum(array_here, hop_no)
+            return array_here
+
+        moments = handle_members_all(moments)
         updated = moments / total_pixels - 3.0 * unmixing
         gram = jnp.dot(updated, updated.T, precision=lax.Precision.HIGHEST)
         unmixing = jnp.dot(inverse_root(gram), updated, precision=lax.Precision.HIGHEST)

time: 395 us -> 375 us (0.949)
  waiting for transfers between devices: 256 us -> 237 us
    psum x2 -> x4, waiting for transfers between devices: 247 us -> 227 us  [handle_members_all(): array_here = lax.psum(array_here, hop_no)]
  transfers between devices with their start and end apart: 7 -> 9, of which waited for: 4 -> 6; matrix products, arithmetic and copies ran while one was open for 3% -> 4% of each run, Pallas kernels for 0% -> 0%
where the time goes in v1:
time: 375 us
  waiting for transfers between devices  237 us (63%)
  matrix products  45.3 us (12%)
  blocking collectives  35.3 us (9%)
  local copies, waits for them, and re-layouts  27 us (7%)
  between operations  15.6 us (4%)
  starting transfers between devices  14.5 us (4%)
    psum x4, waiting for transfers between devices, handle_members_all(): array_here = lax.psum(array_here, hop_no)  227 us
    psum x1, blocking collectives, shards(): lax.psum(jnp.sum(smoothed, axis=(1, 2), dtype=jnp.float32), ('row', 'col'))  30.9 us
    dot_general x1, matrix products, shards(): jnp.einsum('cim,cjm->cij', widened, band_cols, preferred_element_type=jnp...  17 us
    ppermute x2, starting transfers between devices, with_halo(): lax.ppermute(tail, axis, [(i, (i + 1) % count) for i in range(ends)])  8 us
  transfers between devices with their start and end apart: 9, of which 6 were waited for; matrix products, arithmetic and copies ran while one was open for 4% of the time, Pallas kernels for 0%

profile of v1, /device:TPU:0, one launch (start us, length us, event | category | flops | bytes accessed | tf_op | source)
XLA Modules:
  0.0 374.6 jit_solution(1506085563751010675)
XLA Ops:
  7.2 1.3 fusion.76
  8.5 5.0 %collective-permute-start = (bf16[256,8,128]{2,1,0:T(8,128)(2,1)S(1)}, bf16[256,8,128]{2,1,0:T(8,128)(2,1)S(1)}, u32[]{:S(2)}, u32[]{:S(2)}) collective-permute-start(bf16[256,8,128]{2,1,0:T(8,128)(2,1)S(1)} %get-tuple-element.4), channel_id=1, source_target_pairs={{0,4},{4,8},{8,12},{1,5},{5,9},{9,13},{2,6},{6,10},{10,14},{3,7},{... | collective-permute-start | bytes 1572872 | tf_op jit(solution)/shard_map/ppermute | solution.py:19
  13.5 1.3 collective-permute-start.1
  15.0 0.4 convolution_convert_fusion.2
  15.4 3.8 %copy.7 = bf16[256,32,48]{2,1,0:T(8,128)(2,1)} copy(bf16[256,32,48]{0,2,1:T(8,128)(2,1)S(1)} %convolution_convert_fusion.2) | data formatting | bytes 1572864 | tf_op jit(solution)/shard_map/convert_element_type | solution.py:40
  19.2 5.4 %collective-permute-done = bf16[256,8,128]{2,1,0:T(8,128)(2,1)S(1)} collective-permute-done((bf16[256,8,128]{2,1,0:T(8,128)(2,1)S(1)}, bf16[256,8,128]{2,1,0:T(8,128)(2,1)S(1)}, u32[]{:S(2)}, u32[]{:S(2)}) %collective-permute-start) | collective-permute-done | bytes 524320 | tf_op jit(solution)/shard_map/ppermute | solution.py:19
  24.6 4.3 %collective-permute-done.1 = bf16[256,8,128]{2,1,0:T(8,128)(2,1)} collective-permute-done((bf16[256,8,128]{2,1,0:T(8,128)(2,1)S(1)}, bf16[256,8,128]{2,1,0:T(8,128)(2,1)}, u32[]{:S(2)}, u32[]{:S(2)}) %collective-permute-start.1) | collective-permute-done | bytes 524320 | tf_op jit(solution)/shard_map/ppermute | solution.py:21
  28.9 3.3 fusion.13
  32.2 2.9 fusion.75
  35.1 2.7 copy.8
  37.8 2.7 copy.9
  40.5 1.3 collective-permute-start.3
  41.8 3.0 collective-permute-start.2
  44.9 5.2 %convolution_convert_fusion = bf16[256,128,144]{1,0,2:T(8,128)(2,1)} fusion(s32[128,144]{0,1:T(8,128)S(1)} %iota_subtract_fusion, f32[256]{0:T(256)S(1)} %fusion.55, f32[256]{0:T(256)S(1)} %multiply_multiply_fusion.2, f32[17]{0:T(128)S(1)} %multiply_negate_fusion), kind=kOutput, calls=%fused_computation.2 | convolution fusion | flops 165477120 | bytes 9513028 | tf_op jit(solution)/shard_map/ijk,ck->cij/dot_general | solution.py:40
  50.1 3.7 copy.10
  53.8 3.7 copy.11
  57.5 17.0 %convert_reduce_fusion = (f32[256]{0:T(256)S(1)}, bf16[256,32,128]{2,1,0:T(8,128)(2,1)}) fusion(bf16[256,128,144]{1,0,2:T(8,128)(2,1)} %convolution_convert_fusion, bf16[256,32,8]{2,1,0:T(8,128)(2,1)} %copy.11, bf16[256,32,128]{2,1,0:T(8,128)(2,1)S(1)} %fusion.13, bf16[256,32,8]{2,1,0:T(8,128)(2,1)} %copy.10), kind=kOutput, calls=%fused_computation.9 | convolution fusion | flops 312213248 | bytes 13894656 | tf_op jit(solution)/shard_map/cim,cjm->cij/dot_general | solution.py:75
  74.4 2.5 all_to_all.14
  77.0 2.2 copy.13
  79.2 3.8 %all-to-all-start = ((bf16[256,2,2048]{2,0,1:T(8,128)(2,1)}), bf16[256,2,2048]{2,0,1:T(8,128)(2,1)S(1)}, u32[]{:S(2)}, u32[]{:S(2)}) async-start(bf16[256,2,2048]{2,0,1:T(8,128)(2,1)} %copy.13), calls=%async_computation | async-start | bytes 4194304 | tf_op jit(solution)/shard_map/all_to_all | solution.py:80
  83.0 30.9 %psum.35 = f32[256]{0:T(256)S(1)} all-reduce(f32[256]{0:T(256)S(1)} %get-tuple-element.6), channel_id=1, replica_groups=mesh['freq'=2,'row'=4,'col'=4] {'row','col'}, use_global_device_ids=true, to_apply=%region_2.0 | all-reduce | flops 256 | bytes 2048 | tf_op jit(solution)/shard_map/psum | solution.py:78
  113.9 4.5 %all-gather = f32[2,1,256]{2,1,0:T(1,128)S(1)} all-gather(f32[1,1,256]{2,1,0:T(1,128)S(1)} %bitcast.82), channel_id=1, replica_groups=mesh['freq'=2,'row'=4,'col'=4] {'freq'}, dimensions={0}, use_global_device_ids=true | all-gather | bytes 3072 | tf_op jit(solution)/shard_map/all_gather | solution.py:83
  118.3 0.5 fusion.77
  118.8 1.3 copy-done.2
  120.2 2.9 subtract_convert_fusion
  123.2 1.9 fusion.22
  125.1 86.3 %all-reduce.5.cloned.1.call-done = f32[128,512]{1,0:T(8,128)} async-done(((f32[128,512]{1,0:T(8,128)}), f32[128,512]{1,0:T(8,128)}) %all-reduce.5.cloned.1.call-update) | async-done | bytes 262160 | tf_op jit(solution)/shard_map/psum | solution.py:95
  211.5 25.9 %all-reduce.7.cloned.1.call-done = f32[128,512]{1,0:T(8,128)} async-done(((f32[128,512]{1,0:T(8,128)}), f32[128,512]{1,0:T(8,128)}) %all-reduce.7.cloned.1.call-update) | async-done | bytes 262160 | tf_op jit(solution)/shard_map/psum | solution.py:95
  237.4 2.1 multiply_reduce_fusion.1
  240.2 0.2 fusion.32
  240.4 0.2 fusion.53
  240.6 0.2 fusion.52
  240.8 0.2 fusion.31
  241.0 0.2 fusion.79
  241.3 0.2 fusion.78
  241.5 0.2 fusion.30
  241.7 0.2 fusion.81
  241.9 0.2 fusion.80
  242.1 0.2 fusion.29
  242.3 0.2 fusion.82
  242.5 0.2 fusion.83
  242.7 0.2 fusion.28
  242.9 0.2 convolution_divide_fusion.1
  243.2 0.4 fusion.47
  243.6 1.8 fusion.35
  245.4 88.8 %all-reduce.9.cloned.1.call-done = f32[128,512]{1,0:T(8,128)} async-done(((f32[128,512]{1,0:T(8,128)}), f32[128,512]{1,0:T(8,128)}) %all-reduce.9.cloned.1.call-update) | async-done | bytes 262160 | tf_op jit(solution)/shard_map/psum | solution.py:95
  334.3 25.9 %all-reduce.11.cloned.1.call-done = f32[128,512]{1,0:T(8,128)} async-done(((f32[128,512]{1,0:T(8,128)}), f32[128,512]{1,0:T(8,128)}) %all-reduce.11.cloned.1.call-update) | async-done | bytes 262160 | tf_op jit(solution)/shard_map/psum | solution.py:95
  360.2 2.1 multiply_reduce_fusion
  363.1 0.2 fusion.27
  363.3 0.2 fusion.54
  363.5 0.2 fusion.51
  363.7 0.2 fusion.26
  363.9 0.2 fusion.85
  364.1 0.2 fusion.84
  364.3 0.2 fusion.25
  364.5 0.2 fusion.87
  364.7 0.2 fusion.86
  364.9 0.2 fusion.24
  365.1 0.2 fusion.88
  365.4 0.2 fusion.89
  365.6 0.2 fusion.23
  365.8 0.2 convolution_divide_fusion
  366.0 0.4 fusion.49
  366.4 1.6 convolution_convert_fusion.1
  (30 shorter events, 0.4 us)
Async XLA Ops:
  7.2 111.2 %copy-start = (bf16[512,512]{1,0:T(8,128)(2,1)S(1)}, bf16[512,512]{1,0:T(8,128)(2,1)}, u32[]{:S(2)}) copy-start(bf16[512,512]{1,0:T(8,128)(2,1)} %param.6) | copy-start | bytes 1572868
  7.2 7.6 %copy-start.6 = (f32[256]{0:T(256)S(1)}, f32[256]{0:T(256)}, u32[]{:S(2)}) copy-start(f32[256]{0:T(256)} %param.5) | copy-start | bytes 3076
  8.5 16.1 %collective-permute-start = (bf16[256,8,128]{2,1,0:T(8,128)(2,1)S(1)}, bf16[256,8,128]{2,1,0:T(8,128)(2,1)S(1)}, u32[]{:S(2)}, u32[]{:S(2)}) collective-permute-start(bf16[256,8,128]{2,1,0:T(8,128)(2,1)S(1)} %get-tuple-element.4), channel_id=1, source_target_pairs={{0,4},{4,8},{8,12},{1,5},{5,9},{9,13},{2,6},{6,10},{10,14},{3,7},{... | collective-permute-start | bytes 1572872 | tf_op jit(solution)/shard_map/ppermute | solution.py:19
  13.5 15.4 %collective-permute-start.1 = (bf16[256,8,128]{2,1,0:T(8,128)(2,1)S(1)}, bf16[256,8,128]{2,1,0:T(8,128)(2,1)}, u32[]{:S(2)}, u32[]{:S(2)}) collective-permute-start(bf16[256,8,128]{2,1,0:T(8,128)(2,1)S(1)} %get-tuple-element.5), channel_id=1, source_target_pairs={{4,0},{8,4},{12,8},{5,1},{9,5},{13,9},{6,2},{10,6},{14,10},{7,3},{... | collective-permute-start | bytes 1572872 | tf_op jit(solution)/shard_map/ppermute | solution.py:21
  40.5 13.3 %collective-permute-start.3 = (bf16[256,32,8]{0,2,1:T(8,128)(2,1)S(1)}, bf16[256,32,8]{0,2,1:T(8,128)(2,1)S(1)}, u32[]{:S(2)}, u32[]{:S(2)}) collective-permute-start(bf16[256,32,8]{0,2,1:T(8,128)(2,1)S(1)} %copy.9), channel_id=1, source_target_pairs={{1,0},{2,1},{3,2},{5,4},{6,5},{7,6},{9,8},{10,9},{11,10},{13,12},{... | collective-permute-start | bytes 393224 | tf_op jit(solution)/shard_map/ppermute | solution.py:21
  41.8 8.2 %collective-permute-start.2 = (bf16[256,32,8]{0,2,1:T(8,128)(2,1)S(1)}, bf16[256,32,8]{0,2,1:T(8,128)(2,1)S(1)}, u32[]{:S(2)}, u32[]{:S(2)}) collective-permute-start(bf16[256,32,8]{0,2,1:T(8,128)(2,1)S(1)} %copy.8), channel_id=1, source_target_pairs={{0,1},{1,2},{2,3},{4,5},{5,6},{6,7},{8,9},{9,10},{10,11},{12,13},{... | collective-permute-start | bytes 393224 | tf_op jit(solution)/shard_map/ppermute | solution.py:19
  79.2 39.6 %all-to-all-start = ((bf16[256,2,2048]{2,0,1:T(8,128)(2,1)}), bf16[256,2,2048]{2,0,1:T(8,128)(2,1)S(1)}, u32[]{:S(2)}, u32[]{:S(2)}) async-start(bf16[256,2,2048]{2,0,1:T(8,128)(2,1)} %copy.13), calls=%async_computation | async-start | bytes 4194304 | tf_op jit(solution)/shard_map/all_to_all | solution.py:80
  83.0 128.4 %all-reduce.5.cloned.1.call-start = ((), (), s32[]{:S(2)}) async-start(), calls=%async_computation.1 | async-start | bytes 524288 | tf_op jit(solution)/shard_map/psum | solution.py:95
  118.8 1.4 copy-start.2
  120.2 3.0 copy-start.1
  125.1 112.3 %all-reduce.7.cloned.1.call-start = ((), (), s32[]{:S(2)}) async-start(), calls=%async_computation.2 | async-start | bytes 524288 | tf_op jit(solution)/shard_map/psum | solution.py:95
  211.4 122.8 %all-reduce.9.cloned.1.call-start = ((), (), s32[]{:S(2)}) async-start(), calls=%async_computation.3 | async-start | bytes 524288 | tf_op jit(solution)/shard_map/psum | solution.py:95
  237.4 5.8 %copy-start.3 = (f32[128,512]{1,0:T(8,128)S(1)}, f32[128,512]{1,0:T(8,128)}, u32[]{:S(2)}) copy-start(f32[128,512]{1,0:T(8,128)} %all-reduce.7.cloned.1.call-done) | copy-start | bytes 786436
  245.4 114.8 %all-reduce.11.cloned.1.call-start = ((), (), s32[]{:S(2)}) async-start(), calls=%async_computation.4 | async-start | bytes 524288 | tf_op jit(solution)/shard_map/psum | solution.py:95
  360.2 5.8 %copy-start.4 = (f32[128,512]{1,0:T(8,128)S(1)}, f32[128,512]{1,0:T(8,128)}, u32[]{:S(2)}) copy-start(f32[128,512]{1,0:T(8,128)} %all-reduce.11.cloned.1.call-done) | copy-start | bytes 786436
  366.4 1.6 copy-start.5
Sparse Core Ops, SparseCore 0:
  125.2 86.1 all-reduce.4
  213.7 23.6 all-reduce.6
  245.5 88.7 all-reduce.8
  336.5 23.6 all-reduce.10
